TPU v7x, 512 devices: a whole 4x8x8 slice. The times are simulated.
512 devices in a mesh: tile: 128 (over z, y, core), freq: 4 (over x).
Axes of the slice: x: 4, y: 8, z: 8, core: 2. Of those that a mesh axis runs over, the one named last changes fastest.
Arguments:
- observed: float32 [4, 4096, 128], P('freq', 'tile'), may hold values from -6 to 6
- factor_u: float32 [2, 4, 4096, 4096], P(None, 'freq', 'tile'), may hold values from -0.03125 to 0.03125
- factor_v: float32 [2, 4, 16384, 1024], P(None, 'freq', 'tile'), may hold values from -0.125 to 0.125
- tile_ranks: int32 [4, 16, 64], P('freq'), may hold values from 16 to 64
Outputs:
- estimate: float32 [16384, 1024], P('tile', 'freq')
- residual: float32 [4, 4096, 128], P('freq', 'tile')
Inputs may be any that keep to these rules, and one draw needn't show every extreme that they name: Columns r >= tile_ranks[f, i, j] of tile (i, j)'s factors are padding and do not enter the kernel.
All inputs are finite; a program needn't handle non-finite values.
Results may differ from a plain program's by a relative error of at most 0.0001.
Values sent between devices are 32-bit elements; how exact they have to be, the bound alone decides.
No kernel may reach another device: no remote copies, remote signals or barrier semaphores. Data moves between devices by JAX's collectives and lax.ppermute only.
A program may use at most 64 MiB of HBM per device.

v0:
```python
import math

import jax
import jax.numpy as jnp
from jax import lax
from jax.sharding import PartitionSpec as P

R = 64
TIMES = 16
LANES = 128

step_size = 0.25
shrink_factor = 0.5
energy_floor = 1e-06
highest = lax.Precision.HIGHEST


def contract(form, left, right):
    return jnp.einsum(form, left, right, precision=highest)


def phases(freq_index, time_index, total_times):
    turn_count = (2 * freq_index[:, None] + 1) * time_index[None, :] % total_times
    angle_rad = turn_count.astype(jnp.float32) * (2.0 * math.pi / total_times)
    weight = 1.0 / math.sqrt(total_times)
    return (jnp.cos(angle_rad) * weight, jnp.sin(angle_rad) * weight)


def local(observed, factor_u, factor_v, tile_ranks):
    tile_count = lax.axis_size("tile")
    freq_count = lax.axis_size("freq")
    position = lax.axis_index("tile")
    freq_pos = lax.axis_index("freq")
    core = position % 2
    column = position // 2
    rows_u = factor_u.shape[2]
    rows_v = factor_v.shape[2]
    row_tiles = factor_v.shape[3] // R
    col_tiles = factor_u.shape[3] // R
    sources = observed.shape[2] // 2
    half = sources // 2
    quarter = half // 2
    chips_per_row_tile = tile_count // row_tiles // 2
    times_here = TIMES // freq_count
    total_times = times_here * freq_count
    entries = rows_v * tile_count * total_times * sources
    chunk = (2 * quarter * R // LANES, LANES)

    pair = [(k, k ^ 1) for k in range(tile_count)]

    def swap(x):
        return lax.ppermute(x, "tile", pair)

    u_own = factor_u[:, 0]
    v_own = factor_v[:, 0]
    obs_own = observed[0]
    u_both = jnp.concatenate([u_own, swap(u_own)], axis=1)
    v_both = jnp.concatenate([v_own, swap(v_own)], axis=1)
    obs_both = jnp.concatenate([obs_own, swap(obs_own)], axis=0)
    obs_split = obs_both.reshape(2 * rows_u, 2, 2, half)
    target = lax.dynamic_index_in_dim(obs_split, core, axis=2, keepdims=False).transpose(1, 2, 0)

    rank_column = lax.dynamic_index_in_dim(tile_ranks[0], column, axis=1, keepdims=False)
    rank_mask = (jnp.arange(R, dtype=jnp.int32)[None, :] < rank_column[:, None]).astype(jnp.float32)

    all_freqs = jnp.arange(freq_count, dtype=jnp.int32)
    all_times = jnp.arange(total_times, dtype=jnp.int32)
    cos_tab, sin_tab = phases(all_freqs, all_times, total_times)

    def adjoint(resid):
        products = contract("dvm,cmk->dcvk", resid, u_both)
        e_re = products[0, 0] + products[1, 1]
        e_im = products[1, 0] - products[0, 1]
        e = jnp.stack([e_re, e_im]).reshape(2, 2, quarter, col_tiles, R)
        outgoing = e.transpose(3, 1, 0, 2, 4).reshape((tile_count,) + chunk)
        incoming = lax.all_to_all(outgoing, "tile", 0, 0, tiled=True)
        gathered = incoming.reshape((row_tiles, chips_per_row_tile, 2) + chunk).sum(axis=1)
        gathered = gathered.reshape(row_tiles, 2, 2, quarter, R) * rank_mask[:, None, None, None, :]
        coeffs = gathered.transpose(2, 1, 3, 0, 4).reshape(2, half, row_tiles * R)
        blocks = contract("dvk,cnk->dcvn", coeffs, v_both)
        g_re = blocks[0, 0] - blocks[1, 1]
        g_im = blocks[1, 0] + blocks[0, 1]
        return jnp.stack([g_re, g_im])

    def all_freq(spectrum):
        outgoing = jnp.broadcast_to(spectrum[None], (freq_count,) + spectrum.shape)
        return lax.all_to_all(outgoing, "freq", 0, 0, tiled=True)

    def to_time(spectra):
        total = 0.0
        for f in range(freq_count):
            total = total + (
                cos_tab[f][:, None, None] * spectra[f, 0][None]
                - sin_tab[f][:, None, None] * spectra[f, 1][None]
            )
        return total

    def threshold_of(update):
        energy = jnp.sum(update * update)
        outgoing = jnp.broadcast_to(energy, (tile_count, 1))
        total = jnp.sum(lax.all_to_all(outgoing, "tile", 0, 0, tiled=True))
        return shrink_factor * jnp.sqrt(total / entries + energy_floor)

    grad1 = adjoint(target)
    update1 = step_size * to_time(all_freq(grad1))
    threshold1 = threshold_of(update1)
    first = update1 - jnp.clip(update1, -threshold1, threshold1)

    cos_q = lax.dynamic_index_in_dim(cos_tab, freq_pos, axis=0, keepdims=False)
    sin_q = lax.dynamic_index_in_dim(sin_tab, freq_pos, axis=0, keepdims=False)
    x_re = jnp.sum(cos_q[:, None, None] * first, axis=0)
    x_im = -jnp.sum(sin_q[:, None, None] * first, axis=0)
    products = contract("dvn,cnk->dcvk", jnp.stack([x_re, x_im]), v_both)
    c_re = products[0, 0] + products[1, 1]
    c_im = products[1, 0] - products[0, 1]
    coeffs = jnp.stack([c_re, c_im]).reshape(2, 2, quarter, row_tiles, R)
    coeffs = coeffs * rank_mask[None, None, None, :, :]
    outgoing = jnp.broadcast_to(
        coeffs.transpose(3, 1, 0, 2, 4)[:, None],
        (row_tiles, chips_per_row_tile, 2, 2, quarter, R),
    ).reshape((tile_count,) + chunk)
    incoming = lax.all_to_all(outgoing, "tile", 0, 0, tiled=True)
    summed = incoming.reshape(col_tiles, 2, 2, quarter, R).transpose(2, 1, 3, 0, 4)
    summed = summed.reshape(2, half, col_tiles * R)
    blocks = contract("dvk,cmk->dcvm", summed, u_both)
    y_re = blocks[0, 0] - blocks[1, 1]
    y_im = blocks[1, 0] + blocks[0, 1]
    residual = jnp.stack([y_re, y_im]) - target

    grad2 = adjoint(residual)
    update2 = first - step_size * to_time(all_freq(grad2))
    threshold2 = threshold_of(update2)
    mine = lax.dynamic_slice_in_dim(update2, freq_pos * times_here, times_here, axis=0)
    mine = mine - jnp.clip(mine, -threshold2, threshold2)
    mine = mine.reshape(times_here, 2, quarter, 2, rows_v)
    own = mine[:, :, :, 0]
    other = swap(mine[:, :, :, 1])
    first_b = jnp.where(core == 0, own, other)
    second_b = jnp.where(core == 0, other, own)
    estimate = jnp.stack([first_b, second_b], axis=2).transpose(4, 0, 1, 2, 3)
    estimate = estimate.reshape(rows_v, times_here * sources)

    res_own = residual[:, :, :rows_u]
    res_other = swap(residual[:, :, rows_u:])
    lo = jnp.where(core == 0, res_own, res_other)
    hi = jnp.where(core == 0, res_other, res_own)
    residual_out = jnp.stack([lo, hi], axis=1).transpose(3, 0, 1, 2).reshape(1, rows_u, 2 * sources)
    return (estimate, residual_out)


def solution(mesh):
    placed = (
        P("freq", "tile", None),
        P(None, "freq", "tile", None),
        P(None, "freq", "tile", None),
        P("freq", None, None),
    )
    return jax.shard_map(
        local,
        mesh=mesh,
        in_specs=placed,
        out_specs=(P("tile", "freq"), P("freq", "tile", None)),
        check_vma=False,
    )
```

profile of v0, /device:TPU:1, one launch (start us, length us, event | category | flops | bytes accessed | tf_op | source)
XLA Modules:
  0.0 256.7 jit_solution(13324234119178148671)
XLA Ops:
  0.6 8.8 %collective-permute-start.1 = (f32[2,32,4096]{2,1,0:T(8,128)}, f32[2,32,4096]{2,1,0:T(8,128)S(1)}, u32[]{:S(2)}, u32[]{:S(2)}) collective-permute-start(f32[2,32,4096]{2,1,0:T(8,128)} %bitcast.215), channel_id=1, source_target_pairs={{0,4},{4,0},{8,12},{12,8},{16,20},{20,16},{24,28},{28,24},{32,36},... | collective-permute-start | bytes 3145736 | tf_op jit(solution)/shard_map/ppermute | solution.py:52
  9.4 1.9 collective-permute-start.2
  11.4 0.8 concatenate.19
  13.0 3.2 %convolution_bitcast_fusion.1 = f32[2,2,32,4096]{3,2,0,1:T(8,128)S(1)} fusion(f32[2,32,4096]{2,1,0:T(8,128)S(1)} %collective-permute-done.1, f32[2,32,4096]{2,1,0:T(8,128)} %bitcast.216, s32[]{:T(128)S(6)} %select_n.94, f32[32,2,2,32]{0,3,1,2:T(8,128)S(1)} %copy.72, f32[32,2,2,32]{0,3,1,2:T(8,128)S(1)} %copy.73), kind=kOutput, calls=%fused_computation.1 | convolution fusion | flops 403181568 | bytes 4227076 | tf_op jit(solution)/shard_map/dvm,cmk->dcvk/dot_general | solution.py:19
  16.2 0.9 slice_add_fusion.1
  18.1 1.5 sub.122
  20.2 1.6 maximum_bitcast_fusion.1
  21.8 2.7 %reshape.382 = f32[128,16,128]{2,1,0:T(8,128)} reshape(f32[64,2,2,16,64]{4,3,2,1,0:T(8,128)} %maximum_bitcast_fusion.1) | data formatting | bytes 2097152 | tf_op jit(solution)/shard_map/reshape | solution.py:75
  24.5 12.2 %all-to-all-start = ((f32[128,16,128]{2,1,0:T(8,128)}), f32[128,16,128]{2,1,0:T(8,128)}, u32[]{:S(2)}, u32[]{:S(2)}) async-start(f32[128,16,128]{2,1,0:T(8,128)} %reshape.382), calls=%async_computation | async-start | bytes 2097152 | tf_op jit(solution)/shard_map/all_to_all | solution.py:76
  36.6 2.9 %collective-permute-start = (f32[2,128,1024]{2,1,0:T(8,128)S(1)}, f32[2,128,1024]{2,1,0:T(8,128)S(1)}, u32[]{:S(2)}, u32[]{:S(2)}) collective-permute-start(f32[2,128,1024]{2,1,0:T(8,128)S(1)} %bitcast.219), channel_id=1, source_target_pairs={{0,4},{4,0},{8,12},{12,8},{16,20},{20,16},{24,28},{28,24},{32,36},... | collective-permute-start | bytes 3145736 | tf_op jit(solution)/shard_map/ppermute | solution.py:52
  39.9 27.2 %all-to-all-done = f32[128,16,128]{2,1,0:T(8,128)} async-done(((f32[128,16,128]{2,1,0:T(8,128)}), f32[128,16,128]{2,1,0:T(8,128)}, u32[]{:S(2)}, u32[]{:S(2)}) %all-to-all-start) | async-done | bytes 1048608 | tf_op jit(solution)/shard_map/all_to_all | solution.py:76
  67.2 1.3 reduce_sum.72
  68.5 1.0 reshape.384
  69.5 1.1 multiply_bitcast_fusion.1
  70.6 1.1 copy.76
  71.7 1.2 reshape.399
  72.9 2.2 fusion.8
  75.8 4.0 %all-to-all-start.1 = ((f32[4,2,32,256]{3,2,1,0:T(8,128)}), f32[4,2,32,256]{3,2,1,0:T(8,128)S(1)}, u32[]{:S(2)}, u32[]{:S(2)}) async-start(f32[4,2,32,256]{3,2,1,0:T(8,128)} %broadcast_in_dim.10), calls=%async_computation.1 | async-start | bytes 524288 | tf_op jit(solution)/shard_map/all_to_all | solution.py:87
  80.4 5.3 %all-to-all-done.1 = f32[4,2,32,256]{3,2,1,0:T(8,128)S(1)} async-done(((f32[4,2,32,256]{3,2,1,0:T(8,128)}), f32[4,2,32,256]{3,2,1,0:T(8,128)S(1)}, u32[]{:S(2)}, u32[]{:S(2)}) %all-to-all-start.1) | async-done | bytes 262176 | tf_op jit(solution)/shard_map/all_to_all | solution.py:87
  86.4 1.9 multiply_reduce_fusion.3
  89.0 18.8 %all_to_all.37 = f32[128,1,1]{2,1,0:T(1,128)S(1)} all-to-all(f32[128,1,1]{2,1,0:T(1,128)S(1)} %broadcast_in_dim.11), channel_id=1, replica_groups=mesh['tile'=128,'freq'=4] {'tile'}, dimensions={0} | all-to-all | bytes 1024 | tf_op jit(solution)/shard_map/all_to_all | solution.py:101
  107.9 0.8 reduce_sum.74
  109.4 1.3 multiply_reduce_fusion.1
  110.8 1.3 multiply_reduce_fusion.2
  112.1 1.5 fusion.7
  114.1 1.6 broadcast_in_dim.12
  115.7 1.8 reshape.386
  117.5 36.8 %all_to_all.38 = f32[128,16,128]{2,1,0:T(8,128)} all-to-all(f32[128,16,128]{2,1,0:T(8,128)S(1)} %reshape.386), channel_id=1, replica_groups=mesh['tile'=128,'freq'=4] {'tile'}, dimensions={0} | all-to-all | bytes 2097152 | tf_op jit(solution)/shard_map/all_to_all | solution.py:122
  154.3 2.7 %reshape.387 = f32[64,2,2,16,64]{4,3,2,1,0:T(8,128)} reshape(f32[128,16,128]{2,1,0:T(8,128)} %all_to_all.38) | data formatting | bytes 2097152 | tf_op jit(solution)/shard_map/reshape | solution.py:123
  157.0 4.1 %copy.81 = f32[2,2,16,64,64]{4,3,2,1,0:T(8,128)} copy(f32[2,2,16,64,64]{4,2,0,1,3:T(8,128)} %bitcast.223) | data formatting | bytes 2097152 | tf_op jit(solution)/shard_map/transpose | solution.py:123
  161.1 3.0 %reshape.401 = f32[2,32,4096,1]{2,1,0,3:T(8,128)} reshape(f32[2,2,16,64,64]{4,3,2,1,0:T(8,128)} %copy.81) | data formatting | bytes 2097152 | tf_op jit(solution)/shard_map/reshape | solution.py:124
  164.1 4.4 %fusion.10 = f32[2,2,32,64]{3,2,1,0:T(8,128)S(1)} fusion(f32[2,32,4096]{2,1,0:T(8,128)S(1)} %collective-permute-done.1, f32[2,32,4096]{2,1,0:T(8,128)S(1)} %bitcast.217, f32[2,32,4096,1]{2,1,0,3:T(8,128)} %reshape.401), kind=kOutput, calls=%fused_computation.16 | convolution fusion | flops 403177472 | bytes 3178496 | tf_op jit(solution)/shard_map/dvk,cmk->dcvm/dot_general | solution.py:19
  168.6 2.0 convolution_bitcast_fusion
  170.6 0.9 slice_add_fusion
  172.6 1.5 sub.137
  174.7 1.6 maximum_bitcast_fusion.2
  176.2 1.8 reshape.389
  178.0 37.2 %all_to_all.39 = f32[128,16,128]{2,1,0:T(8,128)S(1)} all-to-all(f32[128,16,128]{2,1,0:T(8,128)S(1)} %reshape.389), channel_id=1, replica_groups=mesh['tile'=128,'freq'=4] {'tile'}, dimensions={0} | all-to-all | bytes 2097152 | tf_op jit(solution)/shard_map/all_to_all | solution.py:76
  216.7 2.2 fusion.9
  219.6 3.4 %all-to-all-start.5 = ((f32[4,2,32,256]{3,2,1,0:T(8,128)}), f32[4,2,32,256]{3,2,1,0:T(8,128)S(1)}, u32[]{:S(2)}, u32[]{:S(2)}) async-start(f32[4,2,32,256]{3,2,1,0:T(8,128)} %broadcast_in_dim.13), calls=%async_computation.5 | async-start | bytes 524288 | tf_op jit(solution)/shard_map/all_to_all | solution.py:87
  223.1 2.2 collective-permute-start.4
  225.3 3.9 %all-to-all-done.5 = f32[4,2,32,256]{3,2,1,0:T(8,128)S(1)} async-done(((f32[4,2,32,256]{3,2,1,0:T(8,128)}), f32[4,2,32,256]{3,2,1,0:T(8,128)S(1)}, u32[]{:S(2)}, u32[]{:S(2)}) %all-to-all-start.5) | async-done | bytes 262176 | tf_op jit(solution)/shard_map/all_to_all | solution.py:87
  229.3 1.5 multiply_reduce_fusion
  230.9 1.3 broadcast_in_dim.14
  232.2 7.3 %all-to-all-start.6 = ((f32[128,1,1]{2,1,0:T(1,128)}), f32[128,1,1]{2,1,0:T(1,128)S(1)}, u32[]{:S(2)}, u32[]{:S(2)}) async-start(f32[128,1,1]{2,1,0:T(1,128)} %broadcast_in_dim.14), calls=%async_computation.6 | async-start | bytes 131072 | tf_op jit(solution)/shard_map/all_to_all | solution.py:101
  239.5 11.4 %all-to-all-done.6 = f32[128,1,1]{2,1,0:T(1,128)S(1)} async-done(((f32[128,1,1]{2,1,0:T(1,128)}), f32[128,1,1]{2,1,0:T(1,128)S(1)}, u32[]{:S(2)}, u32[]{:S(2)}) %all-to-all-start.6) | async-done | bytes 544 | tf_op jit(solution)/shard_map/all_to_all | solution.py:101
  252.5 2.5 collective-permute-start.3
  255.9 0.8 copy.92
  (109 shorter events, 11.6 us)
Async XLA Ops:
  0.6 38.9 %copy-start = (s32[1,16,64]{2,1,0:T(8,128)S(1)}, s32[1,16,64]{2,1,0:T(8,128)}, u32[]{:S(2)}) copy-start(s32[1,16,64]{2,1,0:T(8,128)} %param.7) | copy-start | bytes 12292
  0.6 12.3 %collective-permute-start.1 = (f32[2,32,4096]{2,1,0:T(8,128)}, f32[2,32,4096]{2,1,0:T(8,128)S(1)}, u32[]{:S(2)}, u32[]{:S(2)}) collective-permute-start(f32[2,32,4096]{2,1,0:T(8,128)} %bitcast.215), channel_id=1, source_target_pairs={{0,4},{4,0},{8,12},{12,8},{16,20},{20,16},{24,28},{28,24},{32,36},... | collective-permute-start | bytes 3145736 | tf_op jit(solution)/shard_map/ppermute | solution.py:52
  9.4 3.3 %collective-permute-start.2 = (f32[32,128]{1,0:T(8,128)}, f32[32,128]{1,0:T(8,128)S(1)}, u32[]{:S(2)}, u32[]{:S(2)}) collective-permute-start(f32[32,128]{1,0:T(8,128)} %bitcast.229), channel_id=1, source_target_pairs={{0,4},{4,0},{8,12},{12,8},{16,20},{20,16},{24,28},{28,24},{32,36},... | collective-permute-start | bytes 49160 | tf_op jit(solution)/shard_map/ppermute | solution.py:52
  12.3 3.8 %copy-start.13 = (f32[32,2,2,32]{0,3,1,2:T(8,128)}, f32[32,2,2,32]{0,3,1,2:T(8,128)S(1)}, u32[]{:S(2)}) copy-start(f32[32,2,2,32]{0,3,1,2:T(8,128)S(1)} %copy.72) | copy-start | bytes 49156
  12.9 3.2 %copy-start.15 = (f32[32,2,2,32]{0,3,1,2:T(8,128)}, f32[32,2,2,32]{0,3,1,2:T(8,128)S(1)}, u32[]{:S(2)}) copy-start(f32[32,2,2,32]{0,3,1,2:T(8,128)S(1)} %copy.73) | copy-start | bytes 49156
  21.8 14.9 %copy-start.2 = (f32[2,1,128,1024]{3,2,1,0:T(8,128)S(1)}, f32[2,1,128,1024]{3,2,1,0:T(8,128)}, u32[]{:S(2)}) copy-start(f32[2,1,128,1024]{3,2,1,0:T(8,128)} %param.6) | copy-start | bytes 3145732
  24.5 42.7 %all-to-all-start = ((f32[128,16,128]{2,1,0:T(8,128)}), f32[128,16,128]{2,1,0:T(8,128)}, u32[]{:S(2)}, u32[]{:S(2)}) async-start(f32[128,16,128]{2,1,0:T(8,128)} %reshape.382), calls=%async_computation | async-start | bytes 2097152 | tf_op jit(solution)/shard_map/all_to_all | solution.py:76
  36.6 36.2 %collective-permute-start = (f32[2,128,1024]{2,1,0:T(8,128)S(1)}, f32[2,128,1024]{2,1,0:T(8,128)S(1)}, u32[]{:S(2)}, u32[]{:S(2)}) collective-permute-start(f32[2,128,1024]{2,1,0:T(8,128)S(1)} %bitcast.219), channel_id=1, source_target_pairs={{0,4},{4,0},{8,12},{12,8},{16,20},{20,16},{24,28},{28,24},{32,36},... | collective-permute-start | bytes 3145736 | tf_op jit(solution)/shard_map/ppermute | solution.py:52
  72.9 39.2 %copy-start.3 = (f32[2,128,1024]{2,1,0:T(8,128)}, f32[2,128,1024]{2,1,0:T(8,128)S(1)}, u32[]{:S(2)}) copy-start(f32[2,128,1024]{2,1,0:T(8,128)S(1)} %collective-permute-done) | copy-start | bytes 3145732
  75.8 9.9 %all-to-all-start.1 = ((f32[4,2,32,256]{3,2,1,0:T(8,128)}), f32[4,2,32,256]{3,2,1,0:T(8,128)S(1)}, u32[]{:S(2)}, u32[]{:S(2)}) async-start(f32[4,2,32,256]{3,2,1,0:T(8,128)} %broadcast_in_dim.10), calls=%async_computation.1 | async-start | bytes 524288 | tf_op jit(solution)/shard_map/all_to_all | solution.py:87
  85.8 0.6 copy-start.5
  85.8 2.5 copy-start.7
  85.8 3.2 %copy-start.9 = (f32[32,256]{1,0:T(8,128)}, f32[32,256]{1,0:T(8,128)S(1)}, u32[]{:S(2)}) copy-start(f32[32,256]{1,0:T(8,128)S(1)} %get-tuple-element.32) | copy-start | bytes 98308
  85.8 3.2 %copy-start.11 = (f32[32,256]{1,0:T(8,128)}, f32[32,256]{1,0:T(8,128)S(1)}, u32[]{:S(2)}) copy-start(f32[32,256]{1,0:T(8,128)S(1)} %get-tuple-element.33) | copy-start | bytes 98308
  161.1 3.0 %copy-start.1 = (f32[2,1,32,4096]{3,2,1,0:T(8,128)S(1)}, f32[2,1,32,4096]{3,2,1,0:T(8,128)}, u32[]{:S(2)}) copy-start(f32[2,1,32,4096]{3,2,1,0:T(8,128)} %param.5) | copy-start | bytes 3145732
  164.1 4.4 %copy-start.14 = (f32[32,2,2,32]{0,3,1,2:T(8,128)S(1)}, f32[32,2,2,32]{0,3,1,2:T(8,128)}, u32[]{:S(2)}) copy-start(f32[32,2,2,32]{0,3,1,2:T(8,128)} %copy-done.13) | copy-start | bytes 49156
  164.1 4.4 %copy-start.16 = (f32[32,2,2,32]{0,3,1,2:T(8,128)S(1)}, f32[32,2,2,32]{0,3,1,2:T(8,128)}, u32[]{:S(2)}) copy-start(f32[32,2,2,32]{0,3,1,2:T(8,128)} %copy-done.15) | copy-start | bytes 49156
  168.6 2.0 copy-start.17
  215.3 1.2 copy-start.4
  215.9 7.1 %copy-start.18 = (f32[2,32,64]{2,1,0:T(8,128)S(1)}, f32[2,32,64]{2,1,0:T(8,128)}, u32[]{:S(2)}) copy-start(f32[2,32,64]{2,1,0:T(8,128)} %copy-done.17) | copy-start | bytes 49156
  216.6 12.7 %copy-start.6 = (f32[32,256]{1,0:T(8,128)S(1)}, f32[32,256]{1,0:T(8,128)}, u32[]{:S(2)}) copy-start(f32[32,256]{1,0:T(8,128)} %copy-done.5) | copy-start | bytes 98308
  216.6 12.7 %copy-start.8 = (f32[32,256]{1,0:T(8,128)S(1)}, f32[32,256]{1,0:T(8,128)}, u32[]{:S(2)}) copy-start(f32[32,256]{1,0:T(8,128)} %copy-done.7) | copy-start | bytes 98308
  216.6 12.7 %copy-start.10 = (f32[32,256]{1,0:T(8,128)S(1)}, f32[32,256]{1,0:T(8,128)}, u32[]{:S(2)}) copy-start(f32[32,256]{1,0:T(8,128)} %copy-done.9) | copy-start | bytes 98308
  216.6 12.7 %copy-start.12 = (f32[32,256]{1,0:T(8,128)S(1)}, f32[32,256]{1,0:T(8,128)}, u32[]{:S(2)}) copy-start(f32[32,256]{1,0:T(8,128)} %copy-done.11) | copy-start | bytes 98308
  216.6 12.7 %copy-start.19 = (f32[16]{0:T(128)S(1)}, f32[16]{0:T(128)}, u32[]{:S(2)}) copy-start(f32[16]{0:T(128)} %get-tuple-element.43) | copy-start | bytes 196
  216.6 12.7 %copy-start.20 = (f32[16]{0:T(128)S(1)}, f32[16]{0:T(128)}, u32[]{:S(2)}) copy-start(f32[16]{0:T(128)} %get-tuple-element.44) | copy-start | bytes 196
  216.6 12.7 %copy-start.21 = (f32[16]{0:T(128)S(1)}, f32[16]{0:T(128)}, u32[]{:S(2)}) copy-start(f32[16]{0:T(128)} %get-tuple-element.45) | copy-start | bytes 196
  216.6 12.7 %copy-start.22 = (f32[16]{0:T(128)S(1)}, f32[16]{0:T(128)}, u32[]{:S(2)}) copy-start(f32[16]{0:T(128)} %get-tuple-element.46) | copy-start | bytes 196
  216.6 12.7 %copy-start.23 = (f32[16]{0:T(128)S(1)}, f32[16]{0:T(128)}, u32[]{:S(2)}) copy-start(f32[16]{0:T(128)} %get-tuple-element.54) | copy-start | bytes 196
  216.6 12.7 %copy-start.24 = (f32[16]{0:T(128)S(1)}, f32[16]{0:T(128)}, u32[]{:S(2)}) copy-start(f32[16]{0:T(128)} %get-tuple-element.55) | copy-start | bytes 196
  216.6 12.7 %copy-start.25 = (f32[16]{0:T(128)S(1)}, f32[16]{0:T(128)}, u32[]{:S(2)}) copy-start(f32[16]{0:T(128)} %get-tuple-element.56) | copy-start | bytes 196
  216.6 12.7 %copy-start.26 = (f32[16]{0:T(128)S(1)}, f32[16]{0:T(128)}, u32[]{:S(2)}) copy-start(f32[16]{0:T(128)} %get-tuple-element.58) | copy-start | bytes 196
  219.6 9.6 %all-to-all-start.5 = ((f32[4,2,32,256]{3,2,1,0:T(8,128)}), f32[4,2,32,256]{3,2,1,0:T(8,128)S(1)}, u32[]{:S(2)}, u32[]{:S(2)}) async-start(f32[4,2,32,256]{3,2,1,0:T(8,128)} %broadcast_in_dim.13), calls=%async_computation.5 | async-start | bytes 524288 | tf_op jit(solution)/shard_map/all_to_all | solution.py:87
  223.1 16.4 %collective-permute-start.4 = (f32[2,32,32]{2,1,0:T(8,128)S(1)}, f32[2,32,32]{2,1,0:T(8,128)S(1)}, u32[]{:S(2)}, u32[]{:S(2)}) collective-permute-start(f32[2,32,32]{2,1,0:T(8,128)S(1)} %slice.275), channel_id=1, source_target_pairs={{0,4},{4,0},{8,12},{12,8},{16,20},{20,16},{24,28},{28,24},{32,36},... | collective-permute-start | bytes 24584 | tf_op jit(solution)/shard_map/ppermute | solution.py:52
  232.2 18.7 %all-to-all-start.6 = ((f32[128,1,1]{2,1,0:T(1,128)}), f32[128,1,1]{2,1,0:T(1,128)S(1)}, u32[]{:S(2)}, u32[]{:S(2)}) async-start(f32[128,1,1]{2,1,0:T(1,128)} %broadcast_in_dim.14), calls=%async_computation.6 | async-start | bytes 131072 | tf_op jit(solution)/shard_map/all_to_all | solution.py:101
  252.5 3.4 %collective-permute-start.3 = (f32[4,2,16,128]{3,2,1,0:T(8,128)S(1)}, f32[4,2,16,128]{3,2,1,0:T(8,128)S(1)}, u32[]{:S(2)}, u32[]{:S(2)}) collective-permute-start(f32[4,2,16,128]{3,2,1,0:T(8,128)S(1)} %bitcast.228), channel_id=1, source_target_pairs={{0,4},{4,0},{8,12},{12,8},{16,20},{20,16},{24,28},{28,24},{32,36},... | collective-permute-start | bytes 196616 | tf_op jit(solution)/shard_map/ppermute | solution.py:52
where the time goes:
time: 258 us; the launch traced here: 257 us
  blocking collectives  92.8 us (36%)
  waiting for transfers between devices  48.2 us (19%)
  starting transfers between devices  45.1 us (17%)
  local copies, waits for them, and re-layouts  36.6 us (14%)
  other arithmetic  15.6 us (6%)
  matrix products  15.4 us (6%)
  between operations  2.88 us (1%)
    all_to_all x1, blocking collectives, adjoint(): incoming = lax.all_to_all(outgoing, 'tile', 0, 0, tiled=True)  37.2 us
    all_to_all x1, blocking collectives, local(): incoming = lax.all_to_all(outgoing, 'tile', 0, 0, tiled=True)  36.8 us
    all_to_all x1, waiting for transfers between devices, adjoint(): incoming = lax.all_to_all(outgoing, 'tile', 0, 0, tiled=True)  27.2 us
    all_to_all x1, blocking collectives, threshold_of(): total = jnp.sum(lax.all_to_all(outgoing, 'tile', 0, 0, tiled=True))  18.8 us
    ppermute x5, starting transfers between devices, swap(): return lax.ppermute(x, 'tile', pair)  18.3 us
    dot_general x6, matrix products, contract(): return jnp.einsum(form, left, right, precision=highest)  15.4 us
    all_to_all x1, starting transfers between devices, adjoint(): incoming = lax.all_to_all(outgoing, 'tile', 0, 0, tiled=True)  12.2 us
    all_to_all x1, waiting for transfers between devices, threshold_of(): total = jnp.sum(lax.all_to_all(outgoing, 'tile', 0, 0, tiled=True))  11.4 us
  transfers between devices with their start and end apart: 9, of which 5 were waited for; matrix products, arithmetic and copies ran while one was open for 4% of the time, Pallas kernels for 0%

commit v1 on v0

--- a/solution.py
+++ b/solution.py
@@ -12,11 +12,11 @@
 step_size = 0.25
 shrink_factor = 0.5
 energy_floor = 1e-06
-highest = lax.Precision.HIGHEST
+matmul_precision = lax.Precision.HIGH
 
 
 def contract(form, left, right):
-    return jnp.einsum(form, left, right, precision=highest)
+    return jnp.einsum(form, left, right, precision=matmul_precision)
 
 
 def phases(freq_index, time_index, total_times):
@@ -54,7 +54,8 @@
     u_own = factor_u[:, 0]
     v_own = factor_v[:, 0]
     obs_own = observed[0]
-    u_both = jnp.concatenate([u_own, swap(u_own)], axis=1)
+    u_other = swap(u_own)
+    u_both = jnp.concatenate([u_own, u_other], axis=1)
     v_both = jnp.concatenate([v_own, swap(v_own)], axis=1)
     obs_both = jnp.concatenate([obs_own, swap(obs_own)], axis=0)
     obs_split = obs_both.reshape(2 * rows_u, 2, 2, half)
@@ -67,8 +68,13 @@
     all_times = jnp.arange(total_times, dtype=jnp.int32)
     cos_tab, sin_tab = phases(all_freqs, all_times, total_times)
 
-    def adjoint(resid):
-        products = contract("dvm,cmk->dcvk", resid, u_both)
+    def adjoint(resid, split_rows=False):
+        if split_rows:
+            products = contract("dvm,cmk->dcvk", resid[:, :, :rows_u], u_own) + contract(
+                "dvm,cmk->dcvk", resid[:, :, rows_u:], u_other
+            )
+        else:
+            products = contract("dvm,cmk->dcvk", resid, u_both)
         e_re = products[0, 0] + products[1, 1]
         e_im = products[1, 0] - products[0, 1]
         e = jnp.stack([e_re, e_im]).reshape(2, 2, quarter, col_tiles, R)
@@ -101,7 +107,7 @@
         total = jnp.sum(lax.all_to_all(outgoing, "tile", 0, 0, tiled=True))
         return shrink_factor * jnp.sqrt(total / entries + energy_floor)
 
-    grad1 = adjoint(target)
+    grad1 = adjoint(target, split_rows=True)
     update1 = step_size * to_time(all_freq(grad1))
     threshold1 = threshold_of(update1)
     first = update1 - jnp.clip(update1, -threshold1, threshold1)

time: 258 us -> 253 us (0.981)
  matrix products: 15.4 us -> 9.99 us
    dot_general x6 -> x7, matrix products: 15.4 us -> 9.99 us  [contract(): return jnp.einsum(form, left, right, precision=matmul_precision)]
  transfers between devices with their start and end apart: 9 -> 9, of which waited for: 5 -> 5; matrix products, arithmetic and copies ran while one was open for 4% -> 5% of each run, Pallas kernels for 0% -> 0%
where the time goes in v1:
time: 253 us; the launch traced here: 251 us
  blocking collectives  93.1 us (37%)
  waiting for transfers between devices  48.3 us (19%)
  starting transfers between devices  45.1 us (18%)
  local copies, waits for them, and re-layouts  36.4 us (14%)
  other arithmetic  15.6 us (6%)
  matrix products  9.99 us (4%)
  between operations  2.81 us (1%)
    all_to_all x1, blocking collectives, adjoint(): incoming = lax.all_to_all(outgoing, 'tile', 0, 0, tiled=True)  37.4 us
    all_to_all x1, blocking collectives, local(): incoming = lax.all_to_all(outgoing, 'tile', 0, 0, tiled=True)  36.8 us
    all_to_all x1, waiting for transfers between devices, adjoint(): incoming = lax.all_to_all(outgoing, 'tile', 0, 0, tiled=True)  27.2 us
    all_to_all x1, blocking collectives, threshold_of(): total = jnp.sum(lax.all_to_all(outgoing, 'tile', 0, 0, tiled=True))  18.9 us
    ppermute x5, starting transfers between devices, swap(): return lax.ppermute(x, 'tile', pair)  18.3 us
    all_to_all x1, starting transfers between devices, adjoint(): incoming = lax.all_to_all(outgoing, 'tile', 0, 0, tiled=True)  12.2 us
    all_to_all x1, waiting for transfers between devices, threshold_of(): total = jnp.sum(lax.all_to_all(outgoing, 'tile', 0, 0, tiled=True))  11.4 us
    dot_general x7, matrix products, contract(): return jnp.einsum(form, left, right, precision=matmul_precision)  9.99 us
  transfers between devices with their start and end apart: 9, of which 5 were waited for; matrix products, arithmetic and copies ran while one was open for 5% of the time, Pallas kernels for 0%

profile of v1, /device:TPU:1, one launch (start us, length us, event | category | flops | bytes accessed | tf_op | source)
XLA Modules:
  0.0 251.2 jit_solution(13838106061110081476)
XLA Ops:
  0.6 8.8 %collective-permute-start.2 = (f32[2,32,4096]{2,1,0:T(8,128)}, f32[2,32,4096]{2,1,0:T(8,128)S(1)}, u32[]{:S(2)}, u32[]{:S(2)}) collective-permute-start(f32[2,32,4096]{2,1,0:T(8,128)} %bitcast.221), channel_id=1, source_target_pairs={{0,4},{4,0},{8,12},{12,8},{16,20},{20,16},{24,28},{28,24},{32,36},... | collective-permute-start | bytes 3145736 | tf_op jit(solution)/shard_map/ppermute | solution.py:52
  9.4 1.9 collective-permute-start.1
  11.4 0.8 concatenate.18
  13.0 2.2 fusion.15
  15.2 1.1 fusion
  16.3 0.9 slice_add_fusion.1
  18.3 1.5 sub.122
  20.3 1.6 maximum_bitcast_fusion.1
  21.9 2.7 %reshape.382 = f32[128,16,128]{2,1,0:T(8,128)} reshape(f32[64,2,2,16,64]{4,3,2,1,0:T(8,128)} %maximum_bitcast_fusion.1) | data formatting | bytes 2097152 | tf_op jit(solution)/shard_map/reshape | solution.py:81
  24.6 12.2 %all-to-all-start = ((f32[128,16,128]{2,1,0:T(8,128)}), f32[128,16,128]{2,1,0:T(8,128)}, u32[]{:S(2)}, u32[]{:S(2)}) async-start(f32[128,16,128]{2,1,0:T(8,128)} %reshape.382), calls=%async_computation | async-start | bytes 2097152 | tf_op jit(solution)/shard_map/all_to_all | solution.py:82
  36.8 2.9 %collective-permute-start = (f32[2,128,1024]{2,1,0:T(8,128)S(1)}, f32[2,128,1024]{2,1,0:T(8,128)S(1)}, u32[]{:S(2)}, u32[]{:S(2)}) collective-permute-start(f32[2,128,1024]{2,1,0:T(8,128)S(1)} %bitcast.224), channel_id=1, source_target_pairs={{0,4},{4,0},{8,12},{12,8},{16,20},{20,16},{24,28},{28,24},{32,36},... | collective-permute-start | bytes 3145736 | tf_op jit(solution)/shard_map/ppermute | solution.py:52
  40.1 27.2 %all-to-all-done = f32[128,16,128]{2,1,0:T(8,128)} async-done(((f32[128,16,128]{2,1,0:T(8,128)}), f32[128,16,128]{2,1,0:T(8,128)}, u32[]{:S(2)}, u32[]{:S(2)}) %all-to-all-start) | async-done | bytes 1048608 | tf_op jit(solution)/shard_map/all_to_all | solution.py:82
  67.3 1.3 reduce_sum.72
  68.7 1.0 reshape.384
  69.6 1.1 multiply_bitcast_fusion.1
  70.7 1.1 copy.76
  71.8 1.2 reshape.401
  73.0 1.1 fusion.8
  74.9 4.0 %all-to-all-start.1 = ((f32[4,2,32,256]{3,2,1,0:T(8,128)}), f32[4,2,32,256]{3,2,1,0:T(8,128)S(1)}, u32[]{:S(2)}, u32[]{:S(2)}) async-start(f32[4,2,32,256]{3,2,1,0:T(8,128)} %broadcast_in_dim.10), calls=%async_computation.1 | async-start | bytes 524288 | tf_op jit(solution)/shard_map/all_to_all | solution.py:93
  79.5 5.3 %all-to-all-done.1 = f32[4,2,32,256]{3,2,1,0:T(8,128)S(1)} async-done(((f32[4,2,32,256]{3,2,1,0:T(8,128)}), f32[4,2,32,256]{3,2,1,0:T(8,128)S(1)}, u32[]{:S(2)}, u32[]{:S(2)}) %all-to-all-start.1) | async-done | bytes 262176 | tf_op jit(solution)/shard_map/all_to_all | solution.py:93
  85.4 1.9 multiply_reduce_fusion.3
  88.0 18.9 %all_to_all.37 = f32[128,1,1]{2,1,0:T(1,128)S(1)} all-to-all(f32[128,1,1]{2,1,0:T(1,128)S(1)} %broadcast_in_dim.11), channel_id=1, replica_groups=mesh['tile'=128,'freq'=4] {'tile'}, dimensions={0} | all-to-all | bytes 1024 | tf_op jit(solution)/shard_map/all_to_all | solution.py:107
  106.8 0.8 reduce_sum.74
  108.3 1.3 multiply_reduce_fusion.1
  109.6 1.3 multiply_reduce_fusion.2
  112.2 1.6 broadcast_in_dim.12
  113.8 1.8 reshape.386
  115.6 36.8 %all_to_all.38 = f32[128,16,128]{2,1,0:T(8,128)} all-to-all(f32[128,16,128]{2,1,0:T(8,128)S(1)} %reshape.386), channel_id=1, replica_groups=mesh['tile'=128,'freq'=4] {'tile'}, dimensions={0} | all-to-all | bytes 2097152 | tf_op jit(solution)/shard_map/all_to_all | solution.py:128
  152.4 2.7 %reshape.387 = f32[64,2,2,16,64]{4,3,2,1,0:T(8,128)} reshape(f32[128,16,128]{2,1,0:T(8,128)} %all_to_all.38) | data formatting | bytes 2097152 | tf_op jit(solution)/shard_map/reshape | solution.py:129
  155.1 4.1 %copy.81 = f32[2,2,16,64,64]{4,3,2,1,0:T(8,128)} copy(f32[2,2,16,64,64]{4,2,0,1,3:T(8,128)} %bitcast.228) | data formatting | bytes 2097152 | tf_op jit(solution)/shard_map/transpose | solution.py:129
  159.2 3.0 %reshape.404 = f32[2,32,4096,1]{2,1,0,3:T(8,128)} reshape(f32[2,2,16,64,64]{4,3,2,1,0:T(8,128)} %copy.81) | data formatting | bytes 2097152 | tf_op jit(solution)/shard_map/reshape | solution.py:130
  162.2 2.9 %fusion.10 = f32[2,2,32,64]{3,2,1,0:T(8,128)S(1)} fusion(f32[2,32,4096]{2,1,0:T(8,128)S(1)} %collective-permute-done.2, f32[2,32,4096]{2,1,0:T(8,128)S(1)} %bitcast.222, f32[2,32,4096,1]{2,1,0,3:T(8,128)} %reshape.404), kind=kOutput, calls=%fused_computation.16 | convolution fusion | flops 201850880 | bytes 3178496 | tf_op jit(solution)/shard_map/dvk,cmk->dcvm/dot_general | solution.py:19
  165.1 1.0 convolution_bitcast_fusion
  166.1 0.9 slice_add_fusion
  168.0 1.5 sub.137
  170.1 1.6 maximum_bitcast_fusion.2
  171.7 1.8 reshape.389
  173.5 37.4 %all_to_all.39 = f32[128,16,128]{2,1,0:T(8,128)S(1)} all-to-all(f32[128,16,128]{2,1,0:T(8,128)S(1)} %reshape.389), channel_id=1, replica_groups=mesh['tile'=128,'freq'=4] {'tile'}, dimensions={0} | all-to-all | bytes 2097152 | tf_op jit(solution)/shard_map/all_to_all | solution.py:82
  212.3 1.1 fusion.9
  214.1 3.4 %all-to-all-start.5 = ((f32[4,2,32,256]{3,2,1,0:T(8,128)}), f32[4,2,32,256]{3,2,1,0:T(8,128)S(1)}, u32[]{:S(2)}, u32[]{:S(2)}) async-start(f32[4,2,32,256]{3,2,1,0:T(8,128)} %broadcast_in_dim.13), calls=%async_computation.5 | async-start | bytes 524288 | tf_op jit(solution)/shard_map/all_to_all | solution.py:93
  217.6 2.2 collective-permute-start.4
  219.8 3.9 %all-to-all-done.5 = f32[4,2,32,256]{3,2,1,0:T(8,128)S(1)} async-done(((f32[4,2,32,256]{3,2,1,0:T(8,128)}), f32[4,2,32,256]{3,2,1,0:T(8,128)S(1)}, u32[]{:S(2)}, u32[]{:S(2)}) %all-to-all-start.5) | async-done | bytes 262176 | tf_op jit(solution)/shard_map/all_to_all | solution.py:93
  223.9 1.5 multiply_reduce_fusion
  225.4 1.3 broadcast_in_dim.14
  226.7 7.3 %all-to-all-start.6 = ((f32[128,1,1]{2,1,0:T(1,128)}), f32[128,1,1]{2,1,0:T(1,128)S(1)}, u32[]{:S(2)}, u32[]{:S(2)}) async-start(f32[128,1,1]{2,1,0:T(1,128)} %broadcast_in_dim.14), calls=%async_computation.6 | async-start | bytes 131072 | tf_op jit(solution)/shard_map/all_to_all | solution.py:107
  234.0 11.4 %all-to-all-done.6 = f32[128,1,1]{2,1,0:T(1,128)S(1)} async-done(((f32[128,1,1]{2,1,0:T(1,128)}), f32[128,1,1]{2,1,0:T(1,128)S(1)}, u32[]{:S(2)}, u32[]{:S(2)}) %all-to-all-start.6) | async-done | bytes 544 | tf_op jit(solution)/shard_map/all_to_all | solution.py:107
  247.0 2.5 collective-permute-start.3
  250.5 0.8 copy.92
  (107 shorter events, 12.3 us)
Async XLA Ops:
  0.6 39.0 %copy-start = (s32[1,16,64]{2,1,0:T(8,128)S(1)}, s32[1,16,64]{2,1,0:T(8,128)}, u32[]{:S(2)}) copy-start(s32[1,16,64]{2,1,0:T(8,128)} %param.7) | copy-start | bytes 12292
  0.6 14.6 %collective-permute-start.2 = (f32[2,32,4096]{2,1,0:T(8,128)}, f32[2,32,4096]{2,1,0:T(8,128)S(1)}, u32[]{:S(2)}, u32[]{:S(2)}) collective-permute-start(f32[2,32,4096]{2,1,0:T(8,128)} %bitcast.221), channel_id=1, source_target_pairs={{0,4},{4,0},{8,12},{12,8},{16,20},{20,16},{24,28},{28,24},{32,36},... | collective-permute-start | bytes 3145736 | tf_op jit(solution)/shard_map/ppermute | solution.py:52
  9.4 3.3 %collective-permute-start.1 = (f32[32,128]{1,0:T(8,128)}, f32[32,128]{1,0:T(8,128)S(1)}, u32[]{:S(2)}, u32[]{:S(2)}) collective-permute-start(f32[32,128]{1,0:T(8,128)} %bitcast.234), channel_id=1, source_target_pairs={{0,4},{4,0},{8,12},{12,8},{16,20},{20,16},{24,28},{28,24},{32,36},... | collective-permute-start | bytes 49160 | tf_op jit(solution)/shard_map/ppermute | solution.py:52
  13.0 3.3 %copy-start.13 = (f32[2,32,64]{2,1,0:T(8,128)}, f32[2,32,64]{2,1,0:T(8,128)S(1)}, u32[]{:S(2)}) copy-start(f32[2,32,64]{2,1,0:T(8,128)S(1)} %fusion.21) | copy-start | bytes 49156
  21.9 14.9 %copy-start.2 = (f32[2,1,128,1024]{3,2,1,0:T(8,128)S(1)}, f32[2,1,128,1024]{3,2,1,0:T(8,128)}, u32[]{:S(2)}) copy-start(f32[2,1,128,1024]{3,2,1,0:T(8,128)} %param.6) | copy-start | bytes 3145732
  24.6 42.7 %all-to-all-start = ((f32[128,16,128]{2,1,0:T(8,128)}), f32[128,16,128]{2,1,0:T(8,128)}, u32[]{:S(2)}, u32[]{:S(2)}) async-start(f32[128,16,128]{2,1,0:T(8,128)} %reshape.382), calls=%async_computation | async-start | bytes 2097152 | tf_op jit(solution)/shard_map/all_to_all | solution.py:82
  36.8 36.2 %collective-permute-start = (f32[2,128,1024]{2,1,0:T(8,128)S(1)}, f32[2,128,1024]{2,1,0:T(8,128)S(1)}, u32[]{:S(2)}, u32[]{:S(2)}) collective-permute-start(f32[2,128,1024]{2,1,0:T(8,128)S(1)} %bitcast.224), channel_id=1, source_target_pairs={{0,4},{4,0},{8,12},{12,8},{16,20},{20,16},{24,28},{28,24},{32,36},... | collective-permute-start | bytes 3145736 | tf_op jit(solution)/shard_map/ppermute | solution.py:52
  73.0 38.0 %copy-start.3 = (f32[2,128,1024]{2,1,0:T(8,128)}, f32[2,128,1024]{2,1,0:T(8,128)S(1)}, u32[]{:S(2)}) copy-start(f32[2,128,1024]{2,1,0:T(8,128)S(1)} %collective-permute-done) | copy-start | bytes 3145732
  74.9 9.9 %all-to-all-start.1 = ((f32[4,2,32,256]{3,2,1,0:T(8,128)}), f32[4,2,32,256]{3,2,1,0:T(8,128)S(1)}, u32[]{:S(2)}, u32[]{:S(2)}) async-start(f32[4,2,32,256]{3,2,1,0:T(8,128)} %broadcast_in_dim.10), calls=%async_computation.1 | async-start | bytes 524288 | tf_op jit(solution)/shard_map/all_to_all | solution.py:93
  84.8 0.6 copy-start.5
  84.8 2.5 copy-start.7
  84.8 3.1 %copy-start.9 = (f32[32,256]{1,0:T(8,128)}, f32[32,256]{1,0:T(8,128)S(1)}, u32[]{:S(2)}) copy-start(f32[32,256]{1,0:T(8,128)S(1)} %get-tuple-element.32) | copy-start | bytes 98308
  84.8 3.1 %copy-start.11 = (f32[32,256]{1,0:T(8,128)}, f32[32,256]{1,0:T(8,128)S(1)}, u32[]{:S(2)}) copy-start(f32[32,256]{1,0:T(8,128)S(1)} %get-tuple-element.33) | copy-start | bytes 98308
  159.2 3.0 %copy-start.1 = (f32[2,1,32,4096]{3,2,1,0:T(8,128)S(1)}, f32[2,1,32,4096]{3,2,1,0:T(8,128)}, u32[]{:S(2)}) copy-start(f32[2,1,32,4096]{3,2,1,0:T(8,128)} %param.5) | copy-start | bytes 3145732
  162.2 2.9 %copy-start.14 = (f32[2,32,64]{2,1,0:T(8,128)S(1)}, f32[2,32,64]{2,1,0:T(8,128)}, u32[]{:S(2)}) copy-start(f32[2,32,64]{2,1,0:T(8,128)} %copy-done.13) | copy-start | bytes 49156
  165.1 1.0 copy-start.15
  211.0 1.2 copy-start.4
  211.5 6.1 %copy-start.16 = (f32[2,32,64]{2,1,0:T(8,128)S(1)}, f32[2,32,64]{2,1,0:T(8,128)}, u32[]{:S(2)}) copy-start(f32[2,32,64]{2,1,0:T(8,128)} %copy-done.15) | copy-start | bytes 49156
  212.2 11.6 %copy-start.6 = (f32[32,256]{1,0:T(8,128)S(1)}, f32[32,256]{1,0:T(8,128)}, u32[]{:S(2)}) copy-start(f32[32,256]{1,0:T(8,128)} %copy-done.5) | copy-start | bytes 98308
  212.2 11.6 %copy-start.8 = (f32[32,256]{1,0:T(8,128)S(1)}, f32[32,256]{1,0:T(8,128)}, u32[]{:S(2)}) copy-start(f32[32,256]{1,0:T(8,128)} %copy-done.7) | copy-start | bytes 98308
  212.2 11.6 %copy-start.10 = (f32[32,256]{1,0:T(8,128)S(1)}, f32[32,256]{1,0:T(8,128)}, u32[]{:S(2)}) copy-start(f32[32,256]{1,0:T(8,128)} %copy-done.9) | copy-start | bytes 98308
  212.2 11.6 %copy-start.12 = (f32[32,256]{1,0:T(8,128)S(1)}, f32[32,256]{1,0:T(8,128)}, u32[]{:S(2)}) copy-start(f32[32,256]{1,0:T(8,128)} %copy-done.11) | copy-start | bytes 98308
  212.2 11.6 %copy-start.17 = (f32[16]{0:T(128)S(1)}, f32[16]{0:T(128)}, u32[]{:S(2)}) copy-start(f32[16]{0:T(128)} %get-tuple-element.43) | copy-start | bytes 196
  212.2 11.6 %copy-start.18 = (f32[16]{0:T(128)S(1)}, f32[16]{0:T(128)}, u32[]{:S(2)}) copy-start(f32[16]{0:T(128)} %get-tuple-element.44) | copy-start | bytes 196
  212.2 11.6 %copy-start.19 = (f32[16]{0:T(128)S(1)}, f32[16]{0:T(128)}, u32[]{:S(2)}) copy-start(f32[16]{0:T(128)} %get-tuple-element.45) | copy-start | bytes 196
  212.2 11.6 %copy-start.20 = (f32[16]{0:T(128)S(1)}, f32[16]{0:T(128)}, u32[]{:S(2)}) copy-start(f32[16]{0:T(128)} %get-tuple-element.46) | copy-start | bytes 196
  212.3 11.6 %copy-start.21 = (f32[16]{0:T(128)S(1)}, f32[16]{0:T(128)}, u32[]{:S(2)}) copy-start(f32[16]{0:T(128)} %get-tuple-element.54) | copy-start | bytes 196
  212.3 11.6 %copy-start.22 = (f32[16]{0:T(128)S(1)}, f32[16]{0:T(128)}, u32[]{:S(2)}) copy-start(f32[16]{0:T(128)} %get-tuple-element.55) | copy-start | bytes 196
  212.3 11.6 %copy-start.23 = (f32[16]{0:T(128)S(1)}, f32[16]{0:T(128)}, u32[]{:S(2)}) copy-start(f32[16]{0:T(128)} %get-tuple-element.56) | copy-start | bytes 196
  212.3 11.6 %copy-start.24 = (f32[16]{0:T(128)S(1)}, f32[16]{0:T(128)}, u32[]{:S(2)}) copy-start(f32[16]{0:T(128)} %get-tuple-element.58) | copy-start | bytes 196
  214.1 9.6 %all-to-all-start.5 = ((f32[4,2,32,256]{3,2,1,0:T(8,128)}), f32[4,2,32,256]{3,2,1,0:T(8,128)S(1)}, u32[]{:S(2)}, u32[]{:S(2)}) async-start(f32[4,2,32,256]{3,2,1,0:T(8,128)} %broadcast_in_dim.13), calls=%async_computation.5 | async-start | bytes 524288 | tf_op jit(solution)/shard_map/all_to_all | solution.py:93
  217.6 16.4 %collective-permute-start.4 = (f32[2,32,32]{2,1,0:T(8,128)S(1)}, f32[2,32,32]{2,1,0:T(8,128)S(1)}, u32[]{:S(2)}, u32[]{:S(2)}) collective-permute-start(f32[2,32,32]{2,1,0:T(8,128)S(1)} %slice.285), channel_id=1, source_target_pairs={{0,4},{4,0},{8,12},{12,8},{16,20},{20,16},{24,28},{28,24},{32,36},... | collective-permute-start | bytes 24584 | tf_op jit(solution)/shard_map/ppermute | solution.py:52
  226.7 18.7 %all-to-all-start.6 = ((f32[128,1,1]{2,1,0:T(1,128)}), f32[128,1,1]{2,1,0:T(1,128)S(1)}, u32[]{:S(2)}, u32[]{:S(2)}) async-start(f32[128,1,1]{2,1,0:T(1,128)} %broadcast_in_dim.14), calls=%async_computation.6 | async-start | bytes 131072 | tf_op jit(solution)/shard_map/all_to_all | solution.py:107
  247.0 3.4 %collective-permute-start.3 = (f32[4,2,16,128]{3,2,1,0:T(8,128)S(1)}, f32[4,2,16,128]{3,2,1,0:T(8,128)S(1)}, u32[]{:S(2)}, u32[]{:S(2)}) collective-permute-start(f32[4,2,16,128]{3,2,1,0:T(8,128)S(1)} %bitcast.233), channel_id=1, source_target_pairs={{0,4},{4,0},{8,12},{12,8},{16,20},{20,16},{24,28},{28,24},{32,36},... | collective-permute-start | bytes 196616 | tf_op jit(solution)/shard_map/ppermute | solution.py:52
